TPU v7x, 128 devices: a whole 4x4x4 slice. The times are simulated.
128 devices in a mesh: req: 16 (over x, z), head: 8 (over y, core).
Axes of the slice: x: 4, y: 4, z: 4, core: 2. Of those that a mesh axis runs over, the one named last changes fastest.
Arguments:
- tokens: bfloat16 [16384, 1536], P('req', 'head'), may hold values from -6 to 6
- new_counts: int32 [16, 4], P('req'), may hold values from 1 to 512, 1024 in all within a row
- kv_cache: bfloat16 [64, 8, 7680, 128], P('req', 'head'), may hold values from -300 to 300
- norm_attn: float32 [1536], replicated, may hold values from 0.1 to 1.9
- query_weight: bfloat16 [1536, 8, 192], P(None, 'head'), may hold values from -0.15625 to 0.15625
- key_value_weight: bfloat16 [1536, 8, 128], P(None, 'head'), may hold values from -0.4375 to 0.4375
- output_weight: bfloat16 [8, 192, 1536], P('head'), may hold values from -0.15625 to 0.15625
- norm_moe: float32 [1536], replicated, may hold values from 0.1 to 1.9
- routes: int32 [16384, 8], P(('req', 'head')), may hold values from 0 to 31, all different within a row; in each aligned block of 128 rows (0 to 127, 128 to 255, ...) at most 64 rows name the same one
- route_gain: float32 [16384, 8], P(('req', 'head')), may hold values from 0.03 to 0.3
- w_gate_up: bfloat16 [32, 1536, 1024], P('req'), may hold values from -0.15625 to 0.15625
- w_down: bfloat16 [32, 512, 1536], P('req'), may hold values from -0.25 to 0.25
Outputs:
- mixed: bfloat16 [16384, 1536], P(('req', 'head'))
Inputs may be any that keep to these rules, and one draw needn't show every extreme that they name: `new_counts`: the 4 counts of one index of req sum to 1024, and one of them is exactly 512. `routes`: the 8 experts of a row differ. In each aligned block of 128 rows (the rows of one device) no expert is named more than 64 times, a bound that some block reaches.
All inputs are finite; a program needn't handle non-finite values.
Results may differ from a plain program's by a relative error of at most 0.019.
Values may be sent and summed in bfloat16 or wider, within the bound.
No kernel may reach another device: no remote copies, remote signals or barrier semaphores. Data moves between devices by JAX's collectives and lax.ppermute only.
A program may use at most 128 MiB of HBM per device.

v0:
```python
import math
import jax
import jax.numpy as jnp
from jax import lax
from jax.sharding import PartitionSpec as P

EXPERTS = 32
TOPK = 8
RATIO = 15
floor_score = -1e30


def norm_rows(value_rows, gain_row):
    mean_square = jnp.mean(value_rows * value_rows, axis=-1, keepdims=True)
    return value_rows * lax.rsqrt(mean_square + 1e-05) * gain_row


def rope_tables(position, head_size):
    half_size = head_size // 2
    inverse = jnp.exp(
        jnp.arange(half_size, dtype=jnp.float32) * (-2.0 * math.log(10000.0) / head_size)
    )
    angles = position.astype(jnp.float32)[:, None] * inverse[None, :]
    angles = jnp.concatenate([angles, angles], axis=1)
    return (jnp.cos(angles), jnp.sin(angles))


def rotate(vectors, cos_part, sin_part):
    half_size = vectors.shape[-1] // 2
    turned = jnp.concatenate([-vectors[..., half_size:], vectors[..., :half_size]], axis=-1)
    return vectors * cos_part + turned * sin_part


def request_layout(counts, token_count, cache_ratio):
    end_rows = jnp.cumsum(counts)
    starts = end_rows - counts
    row_ids = jnp.arange(token_count, dtype=jnp.int32)
    segment = jnp.sum((row_ids[:, None] >= end_rows[None, :]).astype(jnp.int32), axis=1)
    member = (segment[:, None] == jnp.arange(counts.shape[0], dtype=jnp.int32)[None, :]).astype(
        jnp.int32
    )
    row_begin = jnp.sum(member * starts[None, :], axis=1)
    own_count = jnp.sum(member * counts[None, :], axis=1)
    position = cache_ratio * own_count + row_ids - row_begin
    return (starts, position)


def project(normed, query_weight, key_value_weight, position):
    token_count, model_width = normed.shape
    kv_heads = key_value_weight.shape[1]
    head_size = key_value_weight.shape[2] // 2
    group_size = query_weight.shape[2] // head_size
    query = jnp.dot(
        normed, query_weight.reshape(model_width, -1), preferred_element_type=jnp.float32
    )
    query = query.reshape(token_count, kv_heads, group_size, head_size)
    keyval = jnp.dot(
        normed, key_value_weight.reshape(model_width, -1), preferred_element_type=jnp.float32
    )
    keyval = keyval.reshape(token_count, kv_heads, 2 * head_size)
    cos_part, sin_part = rope_tables(position, head_size)
    query = rotate(query, cos_part[:, None, None, :], sin_part[:, None, None, :]).astype(
        jnp.bfloat16
    )
    new_key = rotate(keyval[..., :head_size], cos_part[:, None, :], sin_part[:, None, :]).astype(
        jnp.bfloat16
    )
    new_value = keyval[..., head_size:].astype(jnp.bfloat16)
    return (query, new_key, new_value)


def absorb(carried, scores, usable, value_rows, pattern):
    highest, denominator, numerator = carried
    scores = jnp.where(usable, scores, floor_score)
    new_top = jnp.maximum(highest, jnp.max(scores, axis=-1))
    rescale = jnp.exp(highest - new_top)
    weights = jnp.where(usable, jnp.exp(scores - new_top[..., None]), 0.0)
    denominator = denominator * rescale + jnp.sum(weights, axis=-1)
    numerator = numerator * rescale[..., None] + jnp.einsum(
        pattern, weights.astype(jnp.bfloat16), value_rows, preferred_element_type=jnp.float32
    )
    return (new_top, denominator, numerator)


def local(
    tokens,
    new_counts,
    kv_cache,
    norm_attn,
    query_weight,
    key_value_weight,
    output_weight,
    norm_moe,
    routes,
    route_gain,
    w_gate_up,
    w_down,
):
    whole = lax.all_gather(tokens, "head", axis=1, tiled=True)
    token_count, model_width = whole.shape
    normed = norm_rows(whole.astype(jnp.float32), norm_attn).astype(jnp.bfloat16)
    counts = new_counts[0]
    starts, position = request_layout(counts, token_count, RATIO)
    query, new_key, new_value = project(normed, query_weight, key_value_weight, position)
    kv_heads, group_size, head_size = (query.shape[1], query.shape[2], query.shape[3])
    window = token_count // 2
    key_block = 3 * window
    score_scale = 1.0 / math.sqrt(head_size)
    stat_shape = (kv_heads, group_size, window)

    def one_request(which, result):
        row_begin = starts[which]
        count_here = counts[which]
        cached = RATIO * count_here
        win_start = jnp.minimum(row_begin, token_count - window)
        row_ids = win_start + jnp.arange(window, dtype=jnp.int32)
        inside = (row_ids >= row_begin) & (row_ids < row_begin + count_here)
        q_win = lax.dynamic_slice_in_dim(query, win_start, window, 0)
        k_win = lax.dynamic_slice_in_dim(new_key, win_start, window, 0)
        v_win = lax.dynamic_slice_in_dim(new_value, win_start, window, 0)
        p_win = lax.dynamic_slice_in_dim(position, win_start, window, 0)
        past = lax.dynamic_index_in_dim(kv_cache, which, 0, keepdims=False)

        def key_step(block_index, carried):
            key_piece = lax.dynamic_slice_in_dim(past, block_index * key_block, key_block, 1)
            slot_ids = block_index * key_block + jnp.arange(key_block, dtype=jnp.int32)
            usable = (slot_ids < cached)[None, None, None, :]
            scores = (
                jnp.einsum(
                    "qhgd,hkd->hgqk",
                    q_win,
                    key_piece[..., :head_size],
                    preferred_element_type=jnp.float32,
                )
                * score_scale
            )
            return absorb(carried, scores, usable, key_piece[..., head_size:], "hgqk,hkd->hgqd")

        start_state = (
            jnp.full(stat_shape, floor_score, jnp.float32),
            jnp.zeros(stat_shape, jnp.float32),
            jnp.zeros(stat_shape + (head_size,), jnp.float32),
        )
        block_count = (cached + key_block - 1) // key_block
        carried = lax.fori_loop(0, block_count, key_step, start_state)
        new_ok = (inside[None, :] & (p_win[None, :] <= p_win[:, None]))[None, None, :, :]
        scores = (
            jnp.einsum("qhgd,khd->hgqk", q_win, k_win, preferred_element_type=jnp.float32)
            * score_scale
        )
        highest, denominator, numerator = absorb(carried, scores, new_ok, v_win, "hgqk,khd->hgqd")
        attended = jnp.transpose(numerator / denominator[..., None], (2, 0, 1, 3))
        current = lax.dynamic_slice_in_dim(result, win_start, window, 0)
        update = jnp.where(inside[:, None, None, None], attended, current)
        return lax.dynamic_update_slice_in_dim(result, update, win_start, 0)

    initial = jnp.zeros(query.shape, jnp.float32)
    result = lax.fori_loop(0, counts.shape[0], one_request, initial)
    attn_out = result.astype(jnp.bfloat16).reshape(token_count, -1)
    partial_value = jnp.dot(
        attn_out, output_weight.reshape(-1, model_width), preferred_element_type=jnp.float32
    )
    per_block = routes.shape[0]
    row_start = lax.axis_index("head") * per_block
    summed = lax.psum(partial_value.astype(jnp.bfloat16), "head").astype(jnp.float32)
    attn_rows = lax.dynamic_slice_in_dim(summed, row_start, per_block, 0)
    base_rows = lax.dynamic_slice_in_dim(whole, row_start, per_block, 0)
    resid = base_rows.astype(jnp.float32) + attn_rows
    moe_in = norm_rows(resid, norm_moe).astype(jnp.bfloat16)
    capacity = per_block // 2
    flat_routes = routes.reshape(-1)
    expert_ids = jnp.arange(EXPERTS, dtype=jnp.int32)
    onehot = (flat_routes[:, None] == expert_ids[None, :]).astype(jnp.int32)
    before = jnp.cumsum(onehot, axis=0) - onehot
    rank_in = jnp.sum(before * onehot, axis=1)
    slot_ids = flat_routes * capacity + rank_in
    owners = jnp.arange(per_block * TOPK, dtype=jnp.int32) // TOPK
    table = jnp.full((EXPERTS * capacity,), per_block, jnp.int32).at[slot_ids].set(owners)
    padded = jnp.concatenate([moe_in, jnp.zeros((1, model_width), jnp.bfloat16)], axis=0)
    req_count = lax.axis_size("req")
    per_req = w_down.shape[0]
    ff_width = w_down.shape[1]
    outgoing = padded[table].reshape(req_count, per_req, capacity, model_width)
    gate_up = jnp.einsum(
        "sncd,ndf->sncf",
        lax.all_to_all(outgoing, "req", split_axis=0, concat_axis=0, tiled=True),
        w_gate_up,
        preferred_element_type=jnp.float32,
    )
    hidden = (jax.nn.silu(gate_up[..., :ff_width]) * gate_up[..., ff_width:]).astype(jnp.bfloat16)
    produced = jnp.einsum(
        "sncf,nfd->sncd", hidden, w_down, preferred_element_type=jnp.float32
    ).astype(jnp.bfloat16)
    arrived = lax.all_to_all(produced, "req", split_axis=0, concat_axis=0, tiled=True)
    gathered = arrived.reshape(EXPERTS * capacity, model_width)[slot_ids].astype(jnp.float32)
    gathered = gathered.reshape(per_block, TOPK, model_width)
    moe_sum = jnp.sum(gathered * route_gain[..., None], axis=1)
    return (resid + moe_sum).astype(jnp.bfloat16)


def solution(mesh):
    in_specs = (
        P("req", "head"),
        P("req", None),
        P("req", "head", None, None),
        P(),
        P(None, "head", None),
        P(None, "head", None),
        P("head", None, None),
        P(),
        P(("req", "head"), None),
        P(("req", "head"), None),
        P("req", None, None),
        P("req", None, None),
    )
    out_specs = P(("req", "head"), None)
    return jax.shard_map(local, mesh=mesh, in_specs=in_specs, out_specs=out_specs, check_vma=False)
```

profile of v0, /device:TPU:93, one launch (start us, length us, event | category | flops | bytes accessed | tf_op | source)
XLA Modules:
  0.0 638.0 jit_solution(5013867156348235563)
XLA Ops:
  14.4 23.0 %all-gather.2.cloned.1.call-done = bf16[1024,1536]{0,1:T(8,128)(2,1)} async-done(((bf16[1024,192]{0,1:T(8,128)(2,1)}), bf16[1024,1536]{0,1:T(8,128)(2,1)}) %all-gather.2.cloned.1.call-update) | async-done | bytes 3145744 | tf_op jit(solution)/shard_map/all_gather | solution.py:99
  47.8 255.9 %while.88 = (s32[]{:T(128)}, bf16[1024,1,3,64]{0,3,2,1:T(8,128)(2,1)}, s32[4]{0:T(128)S(1)}, s32[4]{0:T(128)S(1)}, bf16[4,1,7680,128]{3,2,1,0:T(8,128)(2,1)}, /*...) while((s32[]{:T(128)}, ...), condition=%wide.region_12.13_spmd, body=%wide.region_5.12_spmd.sunk | while | flops 847329280 | bytes 89355064 | solution.py:158
  59.2 4.0 copy.67
  65.1 12.6 %while.89 = (s32[]{:T(128)}, f32[1,3,512]{2,1,0:T(4,128)S(1)}, f32[1,3,512]{2,1,0:T(4,128)S(1)}, f32[1,3,512,64]{2,3,1,0:T(8,128)}, s32[]{:T(128)}, /*index=5*/s...) while((s32[]{:T(128)}, f32[1,3,512]{2,1,0:T(4,128)S(1)}, ...), condition=%wide.region_9.9_spmd, body=%wide.region_6.8_spmd.sunk | while | flops 634854912 | bytes 67547888 | solution.py:145
  71.6 6.1 fusion.131
  98.3 4.0 copy.67
  104.2 62.9 %while.89 = (s32[]{:T(128)}, f32[1,3,512]{2,1,0:T(4,128)S(1)}, f32[1,3,512]{2,1,0:T(4,128)S(1)}, f32[1,3,512,64]{2,3,1,0:T(8,128)}, s32[]{:T(128)}, /*index=5*/s...) while((s32[]{:T(128)}, f32[1,3,512]{2,1,0:T(4,128)S(1)}, ...), condition=%wide.region_9.9_spmd, body=%wide.region_6.8_spmd.sunk | while | flops 634854912 | bytes 67547888 | solution.py:145
  110.7 6.1 fusion.131
  123.3 6.1 fusion.131
  135.8 6.1 fusion.131
  148.4 6.1 fusion.131
  161.0 6.1 fusion.131
  193.9 25.1 %while.89 = (s32[]{:T(128)}, f32[1,3,512]{2,1,0:T(4,128)S(1)}, f32[1,3,512]{2,1,0:T(4,128)S(1)}, f32[1,3,512,64]{2,3,1,0:T(8,128)}, s32[]{:T(128)}, /*index=5*/s...) while((s32[]{:T(128)}, f32[1,3,512]{2,1,0:T(4,128)S(1)}, ...), condition=%wide.region_9.9_spmd, body=%wide.region_6.8_spmd.sunk | while | flops 634854912 | bytes 67547888 | solution.py:145
  200.4 6.1 fusion.131
  212.9 6.1 fusion.131
  239.0 4.0 copy.67
  244.9 50.3 %while.89 = (s32[]{:T(128)}, f32[1,3,512]{2,1,0:T(4,128)S(1)}, f32[1,3,512]{2,1,0:T(4,128)S(1)}, f32[1,3,512,64]{2,3,1,0:T(8,128)}, s32[]{:T(128)}, /*index=5*/s...) while((s32[]{:T(128)}, f32[1,3,512]{2,1,0:T(4,128)S(1)}, ...), condition=%wide.region_9.9_spmd, body=%wide.region_6.8_spmd.sunk | while | flops 634854912 | bytes 67547888 | solution.py:145
  251.4 6.1 fusion.131
  263.9 6.1 fusion.131
  276.5 6.1 fusion.131
  289.1 6.1 fusion.131
  307.9 9.0 %reduce-window.11 = s32[32,8,128]{2,1,0:T(8,128)S(1)} reduce-window(s32[32,8,128]{2,1,0:T(8,128)S(1)} %fusion.96, s32[]{:T(128)} %constant.233.clone.1), window={size=1x1x128 pad=0_0x0_0x127_0}, to_apply=%region_15.16 | reduce-window | flops 4161536 | bytes 262148 | tf_op jit(solution)/shard_map/reduce-window.1
  317.4 4.3 scatter_custom_fusion
  324.7 52.1 %all-reduce.3.cloned.1.call-done = bf16[1024,1536]{1,0:T(8,128)(2,1)} async-done(((bf16[1024,1536]{1,0:T(8,128)(2,1)}), bf16[1024,1536]{1,0:T(8,128)(2,1)}) %all-reduce.3.cloned.1.call-update) | async-done | bytes 3145744 | tf_op jit(solution)/shard_map/psum | solution.py:165
  380.0 14.3 %gather_fusion = bf16[2048,1536]{1,0:T(8,128)(2,1)} fusion(bf16[129,1536]{1,0:T(8,128)(2,1)} %concatenate.59, s32[2048]{0:T(1024)S(1)} %fusion.98), kind=kCustom, calls=%fused_computation | custom fusion | bytes 12591104 | tf_op jit(solution)/shard_map/gather | solution.py:183
  394.3 76.3 %all_to_all.10 = bf16[16,2,64,1536]{3,2,1,0:T(8,128)(2,1)S(1)} all-to-all(bf16[16,2,64,1536]{3,2,1,0:T(8,128)(2,1)} %bitcast.290), channel_id=1, replica_groups=mesh['req'=16,'head'=8] {'req'}, dimensions={0} | all-to-all | bytes 12582912 | tf_op jit(solution)/shard_map/all_to_all | solution.py:186
  470.6 10.8 %fusion.70 = f32[16,2,64,1024]{3,2,0,1:T(8,128)} fusion(bf16[2,1536,1024]{2,1,0:T(8,128)(2,1)} %param.26, bf16[16,2,64,1536]{3,2,1,0:T(8,128)(2,1)S(1)} %all_to_all.10), kind=kOutput, calls=%fused_computation.81 | convolution fusion | flops 6442450944 | bytes 20971520 | tf_op jit(solution)/shard_map/sncd,ndf->sncf/dot_general | solution.py:184
  481.4 7.3 %convert_bitcast_fusion = bf16[16,2,64,1536]{3,2,0,1:T(8,128)(2,1)S(1)} fusion(bf16[2,512,1536]{2,1,0:T(8,128)(2,1)S(1)} %copy-done, f32[16,2,64,1024]{3,2,0,1:T(8,128)} %fusion.70), kind=kOutput, calls=%fused_computation.77 | convolution fusion | flops 3230662656 | bytes 17825792 | tf_op jit(solution)/shard_map/sncf,nfd->sncd/dot_general | solution.py:191
  491.8 8.0 %all-to-all-start.1 = ((bf16[16,2,64,1536]{3,2,1,0:T(8,128)(2,1)}), bf16[16,2,64,1536]{3,2,1,0:T(8,128)(2,1)}, u32[]{:S(2)}, u32[]{:S(2)}) async-start(bf16[16,2,64,1536]{3,2,1,0:T(8,128)(2,1)} %copy.52), calls=%async_computation.1 | async-start | bytes 12582912 | tf_op jit(solution)/shard_map/all_to_all | solution.py:194
  500.6 113.0 %all-to-all-done.1 = bf16[16,2,64,1536]{3,2,1,0:T(8,128)(2,1)} async-done(((bf16[16,2,64,1536]{3,2,1,0:T(8,128)(2,1)}), bf16[16,2,64,1536]{3,2,1,0:T(8,128)(2,1)}, u32[]{:S(2)}, u32[]{:S(2)}) %all-to-all-start.1) | async-done | bytes 6291488 | tf_op jit(solution)/shard_map/all_to_all | solution.py:194
  613.6 10.9 %gather_fusion.1 = bf16[1024,1536]{1,0:T(8,128)(2,1)} fusion(bf16[2048,1536]{1,0:T(8,128)(2,1)} %bitcast.54, s32[1024]{0:T(1024)S(1)} %broadcast_clamp_fusion), kind=kCustom, calls=%fused_computation.1 | custom fusion | bytes 6295552 | tf_op jit(solution)/shard_map/gather | solution.py:195
  624.5 4.7 fusion.65
  (242 shorter events, 195.1 us)
Async XLA Ops:
  6.5 474.8 %copy-start = (bf16[2,512,1536]{2,1,0:T(8,128)(2,1)S(1)}, bf16[2,512,1536]{2,1,0:T(8,128)(2,1)}, u32[]{:S(2)}) copy-start(bf16[2,512,1536]{2,1,0:T(8,128)(2,1)} %param.27) | copy-start | bytes 9437188
  6.5 33.5 %copy-start.12 = (f32[1536]{0:T(1024)S(1)}, f32[1536]{0:T(1024)}, u32[]{:S(2)}) copy-start(f32[1536]{0:T(1024)} %param.19) | copy-start | bytes 18436
  6.5 30.9 %all-gather.2.cloned.1.call-start = ((), (), s32[]{:S(2)}) async-start(), calls=%async_computation.2 | async-start | bytes 3538944 | tf_op jit(solution)/shard_map/all_gather | solution.py:99
  7.3 369.5 %all-reduce.3.cloned.1.call-start = ((), (), s32[]{:S(2)}) async-start(), calls=%async_computation.3 | async-start | bytes 6291456 | tf_op jit(solution)/shard_map/psum | solution.py:165
  40.0 3.9 copy-start.3
  40.0 3.9 copy-start.11
  43.9 2.1 copy-start.4
  43.9 2.1 copy-start.5
  44.9 2.8 copy-start.10
  51.5 0.7 copy-start.2
  68.0 3.6 copy-start.1
  90.6 0.7 copy-start.2
  107.0 3.6 copy-start.1
  119.6 3.6 copy-start.1
  132.2 3.6 copy-start.1
  144.8 3.6 copy-start.1
  157.4 3.6 copy-start.1
  180.3 0.7 copy-start.2
  196.7 3.6 copy-start.1
  209.3 3.6 copy-start.1
  231.3 0.7 copy-start.2
  247.7 3.6 copy-start.1
  260.3 3.6 copy-start.1
  272.9 3.6 copy-start.1
  285.5 3.6 copy-start.1
  303.7 3.9 copy-start.8
  303.7 4.1 copy-start.7
  303.7 13.6 %copy-start.6 = (s32[1024]{0:T(1024)S(1)}, s32[1024]{0:T(1024)}, u32[]{:S(2)}) copy-start(s32[1024]{0:T(1024)} %eq.41) | copy-start | bytes 12292
  491.8 8.0 %copy-start.9 = (f32[128,8]{0,1:T(8,128)S(1)}, f32[128,8]{0,1:T(8,128)}, u32[]{:S(2)}) copy-start(f32[128,8]{0,1:T(8,128)} %param.25) | copy-start | bytes 12292
  491.8 121.8 %all-to-all-start.1 = ((bf16[16,2,64,1536]{3,2,1,0:T(8,128)(2,1)}), bf16[16,2,64,1536]{3,2,1,0:T(8,128)(2,1)}, u32[]{:S(2)}, u32[]{:S(2)}) async-start(bf16[16,2,64,1536]{3,2,1,0:T(8,128)(2,1)} %copy.52), calls=%async_computation.1 | async-start | bytes 12582912 | tf_op jit(solution)/shard_map/all_to_all | solution.py:194
Sparse Core Ops, SparseCore 0:
  9.0 28.3 all-gather.1
  307.7 69.0 all-reduce.2
where the time goes:
time: 640 us; the launch traced here: 638 us
  waiting for transfers between devices  189 us (30%)
  matrix products  159 us (25%)
  local copies, waits for them, and re-layouts  105 us (16%)
  other arithmetic  76.7 us (12%)
  blocking collectives  76.3 us (12%)
  between operations  13.7 us (2%)
  loops' own time  10.3 us (2%)
  starting transfers between devices  8.06 us (1%)
    all_to_all x1, waiting for transfers between devices, local(): lax.all_to_all(produced, 'req', split_axis=0, concat_axis=0, tiled=True)  113 us
    dot_general x16, matrix products, absorb(): jnp.einsum(pattern, weights.astype(jnp.bfloat16), value_rows, preferred_e...  85.6 us
    all_to_all x1, blocking collectives, local(): lax.all_to_all(outgoing, 'req', split_axis=0, concat_axis=0, tiled=True)  76.3 us
    psum x1, waiting for transfers between devices, local(): lax.psum(partial_value.astype(jnp.bfloat16), 'head').astype(jnp.float32)  52.1 us
    reduce_sum x16, other arithmetic, absorb(): denominator = denominator * rescale + jnp.sum(weights, axis=-1)  45.4 us
    dot_general x12, matrix products, key_step(): jnp.einsum('qhgd,hkd->hgqk', q_win, key_piece[..., :head_size], preferred...  33.6 us
    dynamic_slice x8, local copies, waits for them, and re-layouts, one_request(): past = lax.dynamic_index_in_dim(kv_cache, which, 0, keepdims=False)  27.9 us
    all_gather x1, waiting for transfers between devices, local(): whole = lax.all_gather(tokens, 'head', axis=1, tiled=True)  23 us
  transfers between devices with their start and end apart: 3, of which 3 were waited for; matrix products, arithmetic and copies ran while one was open for 4% of the time, Pallas kernels for 0%

commit v1 on v0

--- a/solution.py
+++ b/solution.py
@@ -8,6 +8,22 @@
 TOPK = 8
 RATIO = 15
 floor_score = -1e30
+
+
+def pairwise_exchange(array, axis, split, join):
+    ways, here = (lax.axis_size(axis), lax.axis_index(axis))
+    width = array.shape[split] // ways
+    lengths = list(array.shape)
+    lengths[split] = width
+    height = lengths[join]
+    lengths[join] = height * ways
+    full = jnp.zeros(lengths, array.dtype)
+    for mask in range(ways):
+        part = lax.dynamic_slice_in_dim(array, (here ^ mask) * width, width, axis=split)
+        if mask:
+            part = lax.ppermute(part, axis, [(d, d ^ mask) for d in range(ways)])
+        full = lax.dynamic_update_slice_in_dim(full, part, (here ^ mask) * height, axis=join)
+    return full
 
 
 def norm_rows(value_rows, gain_row):
@@ -191,7 +207,7 @@
     produced = jnp.einsum(
         "sncf,nfd->sncd", hidden, w_down, preferred_element_type=jnp.float32
     ).astype(jnp.bfloat16)
-    arrived = lax.all_to_all(produced, "req", split_axis=0, concat_axis=0, tiled=True)
+    arrived = pairwise_exchange(produced, "req", 0, 0)
     gathered = arrived.reshape(EXPERTS * capacity, model_width)[slot_ids].astype(jnp.float32)
     gathered = gathered.reshape(per_block, TOPK, model_width)
     moe_sum = jnp.sum(gathered * route_gain[..., None], axis=1)

time: 640 us -> 723 us (1.13)
  blocking collectives: 76.3 us -> 0 us
  waiting for transfers between devices: 189 us -> 247 us
  local copies, waits for them, and re-layouts: 105 us -> 159 us
  starting transfers between devices: 8.06 us -> 43.2 us
    all_to_all x1 -> x0, blocking collectives: 76.3 us -> none  [local(): lax.all_to_all(outgoing, 'req', split_axis=0, concat_axis=0, tiled=True)]
    ppermute x0 -> x15, waiting for transfers between devices: none -> 63.9 us  [pairwise_exchange(): part = lax.ppermute(part, axis, [(d, d ^ mask) for d in range(ways)])]
    ppermute x0 -> x15, starting transfers between devices: none -> 36.4 us  [pairwise_exchange(): part = lax.ppermute(part, axis, [(d, d ^ mask) for d in range(ways)])]
    while x44 -> x60, local copies, waits for them, and re-layouts: 11.3 us -> 46 us
    dynamic_update_slice x0 -> x16, local copies, waits for them, and re-layouts: none -> 12.5 us  [pairwise_exchange(): lax.dynamic_update_slice_in_dim(full, part, (here ^ mask) * height, axis=...]
  transfers between devices with their start and end apart: 3 -> 18, of which waited for: 3 -> 13; matrix products, arithmetic and copies ran while one was open for 4% -> 6% of each run, Pallas kernels for 0% -> 0%
where the time goes in v1:
time: 723 us; the launch traced here: 715 us
  waiting for transfers between devices  247 us (34%)
  matrix products  164 us (23%)
  local copies, waits for them, and re-layouts  159 us (22%)
  other arithmetic  77.2 us (11%)
  starting transfers between devices  43.2 us (6%)
  between operations  13.7 us (2%)
  loops' own time  11 us (2%)
    all_to_all x1, waiting for transfers between devices, local(): lax.all_to_all(outgoing, 'req', split_axis=0, concat_axis=0, tiled=True)  108 us
    dot_general x16, matrix products, absorb(): jnp.einsum(pattern, weights.astype(jnp.bfloat16), value_rows, preferred_e...  88.6 us
    ppermute x15, waiting for transfers between devices, pairwise_exchange(): part = lax.ppermute(part, axis, [(d, d ^ mask) for d in range(ways)])  63.9 us
    psum x1, waiting for transfers between devices, local(): lax.psum(partial_value.astype(jnp.bfloat16), 'head').astype(jnp.float32)  52.1 us
    while x60, local copies, waits for them, and re-layouts  46 us
    reduce_sum x16, other arithmetic, absorb(): denominator = denominator * rescale + jnp.sum(weights, axis=-1)  45.2 us
    ppermute x15, starting transfers between devices, pairwise_exchange(): part = lax.ppermute(part, axis, [(d, d ^ mask) for d in range(ways)])  36.4 us
    dot_general x12, matrix products, key_step(): jnp.einsum('qhgd,hkd->hgqk', q_win, key_piece[..., :head_size], preferred...  33.7 us
  transfers between devices with their start and end apart: 18, of which 13 were waited for; matrix products, arithmetic and copies ran while one was open for 6% of the time, Pallas kernels for 0%

profile of v1, /device:TPU:93, one launch (start us, length us, event | category | flops | bytes accessed | tf_op | source)
XLA Modules:
  0.0 714.9 jit_solution(4490140973318029013)
XLA Ops:
  15.0 22.4 %all-gather.2.cloned.1.call-done = bf16[1024,1536]{0,1:T(8,128)(2,1)} async-done(((bf16[1024,192]{0,1:T(8,128)(2,1)}), bf16[1024,1536]{0,1:T(8,128)(2,1)}) %all-gather.2.cloned.1.call-update) | async-done | bytes 3145744 | tf_op jit(solution)/shard_map/all_gather | solution.py:115
  47.6 300.1 %while.88 = (s32[]{:T(128)}, bf16[1024,1,3,64]{0,3,2,1:T(8,128)(2,1)}, s32[4]{0:T(128)}, s32[4]{0:T(128)}, bf16[4,1,7680,128]{3,2,1,0:T(8,128)(2,1)}, /*index=5*...) while((s32[]{:T(128)}, ...), condition=%wide.region_12.13_spmd, body=%wide.region_5.12_spmd.sunk | while | flops 847329280 | bytes 92500848 | solution.py:174
  66.6 15.4 %while.89 = (s32[]{:T(128)}, f32[1,3,512]{2,1,0:T(4,128)S(1)}, f32[1,3,512]{2,1,0:T(4,128)S(1)}, f32[1,3,512,64]{2,3,1,0:T(8,128)}, s32[]{:T(128)}, /*index=5*/s...) while((s32[]{:T(128)}, f32[1,3,512]{2,1,0:T(4,128)S(1)}, ...), condition=%wide.region_9.9_spmd, body=%wide.region_6.8_spmd.sunk | while | flops 634854912 | bytes 67547888 | solution.py:161
  75.9 6.1 fusion.131
  110.9 77.3 %while.89 = (s32[]{:T(128)}, f32[1,3,512]{2,1,0:T(4,128)S(1)}, f32[1,3,512]{2,1,0:T(4,128)S(1)}, f32[1,3,512,64]{2,3,1,0:T(8,128)}, s32[]{:T(128)}, /*index=5*/s...) while((s32[]{:T(128)}, f32[1,3,512]{2,1,0:T(4,128)S(1)}, ...), condition=%wide.region_9.9_spmd, body=%wide.region_6.8_spmd.sunk | while | flops 634854912 | bytes 67547888 | solution.py:161
  120.2 6.1 fusion.131
  135.7 6.1 fusion.131
  151.2 6.1 fusion.131
  166.6 6.1 fusion.131
  182.1 6.1 fusion.131
  217.3 30.9 %while.89 = (s32[]{:T(128)}, f32[1,3,512]{2,1,0:T(4,128)S(1)}, f32[1,3,512]{2,1,0:T(4,128)S(1)}, f32[1,3,512,64]{2,3,1,0:T(8,128)}, s32[]{:T(128)}, /*index=5*/s...) while((s32[]{:T(128)}, f32[1,3,512]{2,1,0:T(4,128)S(1)}, ...), condition=%wide.region_9.9_spmd, body=%wide.region_6.8_spmd.sunk | while | flops 634854912 | bytes 67547888 | solution.py:161
  242.1 6.1 fusion.131
  276.5 61.8 %while.89 = (s32[]{:T(128)}, f32[1,3,512]{2,1,0:T(4,128)S(1)}, f32[1,3,512]{2,1,0:T(4,128)S(1)}, f32[1,3,512,64]{2,3,1,0:T(8,128)}, s32[]{:T(128)}, /*index=5*/s...) while((s32[]{:T(128)}, f32[1,3,512]{2,1,0:T(4,128)S(1)}, ...), condition=%wide.region_9.9_spmd, body=%wide.region_6.8_spmd.sunk | while | flops 634854912 | bytes 67547888 | solution.py:161
  285.8 6.1 fusion.131
  301.3 6.1 fusion.131
  316.7 6.1 fusion.131
  332.2 6.1 fusion.131
  351.8 9.0 %reduce-window.11 = s32[32,8,128]{2,1,0:T(8,128)S(1)} reduce-window(s32[32,8,128]{2,1,0:T(8,128)S(1)} %fusion.96, s32[]{:T(128)} %constant.252.clone.1), window={size=1x1x128 pad=0_0x0_0x127_0}, to_apply=%region_15.16 | reduce-window | flops 4161536 | bytes 262148 | tf_op jit(solution)/shard_map/reduce-window.1
  368.7 52.1 %all-reduce.3.cloned.1.call-done = bf16[1024,1536]{1,0:T(8,128)(2,1)} async-done(((bf16[1024,1536]{1,0:T(8,128)(2,1)}), bf16[1024,1536]{1,0:T(8,128)(2,1)}) %all-reduce.3.cloned.1.call-update) | async-done | bytes 3145744 | tf_op jit(solution)/shard_map/psum | solution.py:181
  424.0 14.3 %gather_fusion = bf16[2048,1536]{1,0:T(8,128)(2,1)} fusion(bf16[129,1536]{1,0:T(8,128)(2,1)} %concatenate.59, s32[2048]{0:T(1024)S(1)} %fusion.98), kind=kCustom, calls=%fused_computation | custom fusion | bytes 12591104 | tf_op jit(solution)/shard_map/gather | solution.py:199
  438.3 6.8 all-to-all-start
  445.8 107.9 %all-to-all-done = bf16[16,2,64,1536]{3,2,1,0:T(8,128)(2,1)} async-done(((bf16[16,2,64,1536]{3,2,1,0:T(8,128)(2,1)}), bf16[16,2,64,1536]{3,2,1,0:T(8,128)(2,1)}, u32[]{:S(2)}, u32[]{:S(2)}) %all-to-all-start) | async-done | bytes 6291488 | tf_op jit(solution)/shard_map/all_to_all | solution.py:202
  553.8 12.6 %fusion.70 = f32[16,2,64,1024]{3,2,0,1:T(8,128)} fusion(bf16[2,1536,1024]{2,1,0:T(8,128)(2,1)} %param.26, bf16[16,2,64,1536]{3,2,1,0:T(8,128)(2,1)} %all-to-all-done), kind=kOutput, calls=%fused_computation.81 | convolution fusion | flops 6442450944 | bytes 20971520 | tf_op jit(solution)/shard_map/sncd,ndf->sncf/dot_general | solution.py:200
  566.3 7.3 %convolution_convert_fusion = bf16[2,16,64,1536]{3,2,1,0:T(8,128)(2,1)S(1)} fusion(bf16[2,512,1536]{2,1,0:T(8,128)(2,1)S(1)} %copy-done, f32[16,2,64,1024]{3,2,0,1:T(8,128)} %fusion.70), kind=kOutput, calls=%fused_computation.77 | convolution fusion | flops 3230662656 | bytes 17825792 | tf_op jit(solution)/shard_map/sncf,nfd->sncd/dot_general | solution.py:207
  585.7 22.6 %collective-permute-done.1 = bf16[1,2,64,1536]{3,2,1,0:T(8,128)(2,1)S(1)} collective-permute-done((bf16[1,2,64,1536]{3,2,1,0:T(8,128)(2,1)S(1)}, bf16[1,2,64,1536]{3,2,1,0:T(8,128)(2,1)S(1)}, u32[]{:S(2)}, u32[]{:S(2)}) %collective-permute-start.1) | collective-permute-done | bytes 393248 | tf_op jit(solution)/shard_map/ppermute | solution.py:24
  624.8 7.2 %collective-permute-start.12 = (bf16[1,2,64,1536]{3,2,1,0:T(8,128)(2,1)S(1)}, bf16[1,2,64,1536]{3,2,1,0:T(8,128)(2,1)S(1)}, u32[]{:S(2)}, u32[]{:S(2)}) collective-permute-start(bf16[1,2,64,1536]{3,2,1,0:T(8,128)(2,1)S(1)} %get-tuple-element.448), channel_id=1, source_target_pairs={{0,104},{8,96},{16,120},{24,112},{32,72},{40,64},{48,88},{56,80},{... | collective-permute-start | bytes 1179656 | tf_op jit(solution)/shard_map/ppermute | solution.py:24
  641.7 8.5 %collective-permute-start.14 = (bf16[1,2,64,1536]{3,2,1,0:T(8,128)(2,1)S(1)}, bf16[1,2,64,1536]{3,2,1,0:T(8,128)(2,1)S(1)}, u32[]{:S(2)}, u32[]{:S(2)}) collective-permute-start(bf16[1,2,64,1536]{3,2,1,0:T(8,128)(2,1)S(1)} %get-tuple-element.446), channel_id=1, source_target_pairs={{0,120},{8,112},{16,104},{24,96},{32,88},{40,80},{48,72},{56,64},{... | collective-permute-start | bytes 1179656 | tf_op jit(solution)/shard_map/ppermute | solution.py:24
  652.1 11.2 %collective-permute-done.11 = bf16[1,2,64,1536]{3,2,1,0:T(8,128)(2,1)S(1)} collective-permute-done((bf16[1,2,64,1536]{3,2,1,0:T(8,128)(2,1)S(1)}, bf16[1,2,64,1536]{3,2,1,0:T(8,128)(2,1)S(1)}, u32[]{:S(2)}, u32[]{:S(2)}) %collective-permute-start.11) | collective-permute-done | bytes 393248 | tf_op jit(solution)/shard_map/ppermute | solution.py:24
  664.1 7.7 %collective-permute-done.12 = bf16[1,2,64,1536]{3,2,1,0:T(8,128)(2,1)S(1)} collective-permute-done((bf16[1,2,64,1536]{3,2,1,0:T(8,128)(2,1)S(1)}, bf16[1,2,64,1536]{3,2,1,0:T(8,128)(2,1)S(1)}, u32[]{:S(2)}, u32[]{:S(2)}) %collective-permute-start.12) | collective-permute-done | bytes 393248 | tf_op jit(solution)/shard_map/ppermute | solution.py:24
  672.5 7.6 %collective-permute-done.13 = bf16[1,2,64,1536]{3,2,1,0:T(8,128)(2,1)S(1)} collective-permute-done((bf16[1,2,64,1536]{3,2,1,0:T(8,128)(2,1)S(1)}, bf16[1,2,64,1536]{3,2,1,0:T(8,128)(2,1)S(1)}, u32[]{:S(2)}, u32[]{:S(2)}) %collective-permute-start.13) | collective-permute-done | bytes 393248 | tf_op jit(solution)/shard_map/ppermute | solution.py:24
  680.9 8.8 %collective-permute-done.14 = bf16[1,2,64,1536]{3,2,1,0:T(8,128)(2,1)S(1)} collective-permute-done((bf16[1,2,64,1536]{3,2,1,0:T(8,128)(2,1)S(1)}, bf16[1,2,64,1536]{3,2,1,0:T(8,128)(2,1)S(1)}, u32[]{:S(2)}, u32[]{:S(2)}) %collective-permute-start.14) | collective-permute-done | bytes 393248 | tf_op jit(solution)/shard_map/ppermute | solution.py:24
  690.6 10.9 %gather_fusion.1 = bf16[1024,1536]{1,0:T(8,128)(2,1)} fusion(bf16[2048,1536]{1,0:T(8,128)(2,1)} %bitcast.69, s32[1024]{0:T(1024)S(1)} %broadcast_clamp_fusion), kind=kCustom, calls=%fused_computation.1 | custom fusion | bytes 6295552 | tf_op jit(solution)/shard_map/gather | solution.py:211
  (302 shorter events, 306.1 us)
Async XLA Ops:
  6.5 559.8 %copy-start = (bf16[2,512,1536]{2,1,0:T(8,128)(2,1)S(1)}, bf16[2,512,1536]{2,1,0:T(8,128)(2,1)}, u32[]{:S(2)}) copy-start(bf16[2,512,1536]{2,1,0:T(8,128)(2,1)} %param.27) | copy-start | bytes 9437188
  6.5 30.9 %all-gather.2.cloned.1.call-start = ((), (), s32[]{:S(2)}) async-start(), calls=%async_computation.1 | async-start | bytes 3538944 | tf_op jit(solution)/shard_map/all_gather | solution.py:115
  7.3 413.5 %all-reduce.3.cloned.1.call-start = ((), (), s32[]{:S(2)}) async-start(), calls=%async_computation.2 | async-start | bytes 6291456 | tf_op jit(solution)/shard_map/psum | solution.py:181
  40.0 3.9 copy-start.5
  40.0 3.9 copy-start.12
  47.6 17.1 %copy-start.3 = (bf16[1024,1,3,64]{0,3,2,1:T(8,128)(2,1)}, bf16[1024,1,3,64]{0,3,2,1:T(8,128)(2,1)S(1)}, u32[]{:S(2)}) copy-start(bf16[1024,1,3,64]{0,3,2,1:T(8,128)(2,1)S(1)} %get-tuple-element.705) | copy-start | bytes 1179652 | tf_op jit(solution)/shard_map/while
  84.7 7.2 %copy-start.4 = (bf16[1024,1,3,64]{0,3,2,1:T(8,128)(2,1)S(1)}, bf16[1024,1,3,64]{0,3,2,1:T(8,128)(2,1)}, u32[]{:S(2)}) copy-start(bf16[1024,1,3,64]{0,3,2,1:T(8,128)(2,1)} %copy-done.3) | copy-start | bytes 1179652 | tf_op jit(solution)/shard_map/while
  91.9 17.1 %copy-start.3 = (bf16[1024,1,3,64]{0,3,2,1:T(8,128)(2,1)}, bf16[1024,1,3,64]{0,3,2,1:T(8,128)(2,1)S(1)}, u32[]{:S(2)}) copy-start(bf16[1024,1,3,64]{0,3,2,1:T(8,128)(2,1)S(1)} %get-tuple-element.705) | copy-start | bytes 1179652 | tf_op jit(solution)/shard_map/while
  190.9 7.5 %copy-start.4 = (bf16[1024,1,3,64]{0,3,2,1:T(8,128)(2,1)S(1)}, bf16[1024,1,3,64]{0,3,2,1:T(8,128)(2,1)}, u32[]{:S(2)}) copy-start(bf16[1024,1,3,64]{0,3,2,1:T(8,128)(2,1)} %copy-done.3) | copy-start | bytes 1179652 | tf_op jit(solution)/shard_map/while
  198.4 17.0 %copy-start.3 = (bf16[1024,1,3,64]{0,3,2,1:T(8,128)(2,1)}, bf16[1024,1,3,64]{0,3,2,1:T(8,128)(2,1)S(1)}, u32[]{:S(2)}) copy-start(bf16[1024,1,3,64]{0,3,2,1:T(8,128)(2,1)S(1)} %get-tuple-element.705) | copy-start | bytes 1179652 | tf_op jit(solution)/shard_map/while
  251.0 6.6 copy-start.4
  257.6 17.0 %copy-start.3 = (bf16[1024,1,3,64]{0,3,2,1:T(8,128)(2,1)}, bf16[1024,1,3,64]{0,3,2,1:T(8,128)(2,1)S(1)}, u32[]{:S(2)}) copy-start(bf16[1024,1,3,64]{0,3,2,1:T(8,128)(2,1)S(1)} %get-tuple-element.705) | copy-start | bytes 1179652 | tf_op jit(solution)/shard_map/while
  341.0 6.6 copy-start.4
  347.7 4.1 copy-start.9
  347.7 13.6 %copy-start.8 = (s32[1024]{0:T(1024)S(1)}, s32[1024]{0:T(1024)}, u32[]{:S(2)}) copy-start(s32[1024]{0:T(1024)} %eq.41) | copy-start | bytes 12292
  438.3 6.8 copy-start.11
  438.3 115.5 %all-to-all-start = ((bf16[16,2,64,1536]{3,2,1,0:T(8,128)(2,1)}), bf16[16,2,64,1536]{3,2,1,0:T(8,128)(2,1)}, u32[]{:S(2)}, u32[]{:S(2)}) async-start(bf16[16,2,64,1536]{3,2,1,0:T(8,128)(2,1)} %bitcast.320), calls=%async_computation | async-start | bytes 12582912 | tf_op jit(solution)/shard_map/all_to_all | solution.py:202
  574.4 10.6 %collective-permute-start = (bf16[1,2,64,1536]{3,2,1,0:T(8,128)(2,1)S(1)}, bf16[1,2,64,1536]{3,2,1,0:T(8,128)(2,1)S(1)}, u32[]{:S(2)}, u32[]{:S(2)}) collective-permute-start(bf16[1,2,64,1536]{3,2,1,0:T(8,128)(2,1)S(1)} %get-tuple-element.460), channel_id=1, source_target_pairs={{0,8},{8,0},{16,24},{24,16},{32,40},{40,32},{48,56},{56,48},{64,72... | collective-permute-start | bytes 1179656 | tf_op jit(solution)/shard_map/ppermute | solution.py:24
  574.5 33.9 %collective-permute-start.1 = (bf16[1,2,64,1536]{3,2,1,0:T(8,128)(2,1)S(1)}, bf16[1,2,64,1536]{3,2,1,0:T(8,128)(2,1)S(1)}, u32[]{:S(2)}, u32[]{:S(2)}) collective-permute-start(bf16[1,2,64,1536]{3,2,1,0:T(8,128)(2,1)S(1)} %get-tuple-element.459), channel_id=1, source_target_pairs={{0,16},{8,24},{16,0},{24,8},{32,48},{40,56},{48,32},{56,40},{64,80... | collective-permute-start | bytes 1179656 | tf_op jit(solution)/shard_map/ppermute | solution.py:24
  574.6 34.6 %collective-permute-start.2 = (bf16[1,2,64,1536]{3,2,1,0:T(8,128)(2,1)S(1)}, bf16[1,2,64,1536]{3,2,1,0:T(8,128)(2,1)S(1)}, u32[]{:S(2)}, u32[]{:S(2)}) collective-permute-start(bf16[1,2,64,1536]{3,2,1,0:T(8,128)(2,1)S(1)} %get-tuple-element.458), channel_id=1, source_target_pairs={{0,24},{8,16},{16,8},{24,0},{32,56},{40,48},{48,40},{56,32},{64,88... | collective-permute-start | bytes 1179656 | tf_op jit(solution)/shard_map/ppermute | solution.py:24
  577.1 32.8 %collective-permute-start.3 = (bf16[1,2,64,1536]{3,2,1,0:T(8,128)(2,1)S(1)}, bf16[1,2,64,1536]{3,2,1,0:T(8,128)(2,1)S(1)}, u32[]{:S(2)}, u32[]{:S(2)}) collective-permute-start(bf16[1,2,64,1536]{3,2,1,0:T(8,128)(2,1)S(1)} %get-tuple-element.457), channel_id=1, source_target_pairs={{0,32},{8,40},{16,48},{24,56},{32,0},{40,8},{48,16},{56,24},{64,96... | collective-permute-start | bytes 1179656 | tf_op jit(solution)/shard_map/ppermute | solution.py:24
  577.1 37.9 %collective-permute-start.4 = (bf16[1,2,64,1536]{3,2,1,0:T(8,128)(2,1)S(1)}, bf16[1,2,64,1536]{3,2,1,0:T(8,128)(2,1)S(1)}, u32[]{:S(2)}, u32[]{:S(2)}) collective-permute-start(bf16[1,2,64,1536]{3,2,1,0:T(8,128)(2,1)S(1)} %get-tuple-element.456), channel_id=1, source_target_pairs={{0,40},{8,32},{16,56},{24,48},{32,8},{40,0},{48,24},{56,16},{64,10... | collective-permute-start | bytes 1179656 | tf_op jit(solution)/shard_map/ppermute | solution.py:24
  584.9 33.3 %collective-permute-start.5 = (bf16[1,2,64,1536]{3,2,1,0:T(8,128)(2,1)S(1)}, bf16[1,2,64,1536]{3,2,1,0:T(8,128)(2,1)S(1)}, u32[]{:S(2)}, u32[]{:S(2)}) collective-permute-start(bf16[1,2,64,1536]{3,2,1,0:T(8,128)(2,1)S(1)} %get-tuple-element.455), channel_id=1, source_target_pairs={{0,48},{8,56},{16,32},{24,40},{32,16},{40,24},{48,0},{56,8},{64,11... | collective-permute-start | bytes 1179656 | tf_op jit(solution)/shard_map/ppermute | solution.py:24
  608.3 11.6 %collective-permute-start.6 = (bf16[1,2,64,1536]{3,2,1,0:T(8,128)(2,1)S(1)}, bf16[1,2,64,1536]{3,2,1,0:T(8,128)(2,1)S(1)}, u32[]{:S(2)}, u32[]{:S(2)}) collective-permute-start(bf16[1,2,64,1536]{3,2,1,0:T(8,128)(2,1)S(1)} %get-tuple-element.454), channel_id=1, source_target_pairs={{0,56},{8,48},{16,40},{24,32},{32,24},{40,16},{48,8},{56,0},{64,12... | collective-permute-start | bytes 1179656 | tf_op jit(solution)/shard_map/ppermute | solution.py:24
  609.1 15.6 %collective-permute-start.7 = (bf16[1,2,64,1536]{3,2,1,0:T(8,128)(2,1)S(1)}, bf16[1,2,64,1536]{3,2,1,0:T(8,128)(2,1)S(1)}, u32[]{:S(2)}, u32[]{:S(2)}) collective-permute-start(bf16[1,2,64,1536]{3,2,1,0:T(8,128)(2,1)S(1)} %get-tuple-element.453), channel_id=1, source_target_pairs={{0,64},{8,72},{16,80},{24,88},{32,96},{40,104},{48,112},{56,120},{... | collective-permute-start | bytes 1179656 | tf_op jit(solution)/shard_map/ppermute | solution.py:24
  609.9 23.3 %collective-permute-start.8 = (bf16[1,2,64,1536]{3,2,1,0:T(8,128)(2,1)S(1)}, bf16[1,2,64,1536]{3,2,1,0:T(8,128)(2,1)S(1)}, u32[]{:S(2)}, u32[]{:S(2)}) collective-permute-start(bf16[1,2,64,1536]{3,2,1,0:T(8,128)(2,1)S(1)} %get-tuple-element.452), channel_id=1, source_target_pairs={{0,72},{8,64},{16,88},{24,80},{32,104},{40,96},{48,120},{56,112},{... | collective-permute-start | bytes 1179656 | tf_op jit(solution)/shard_map/ppermute | solution.py:24
  614.9 26.8 %collective-permute-start.9 = (bf16[1,2,64,1536]{3,2,1,0:T(8,128)(2,1)S(1)}, bf16[1,2,64,1536]{3,2,1,0:T(8,128)(2,1)S(1)}, u32[]{:S(2)}, u32[]{:S(2)}) collective-permute-start(bf16[1,2,64,1536]{3,2,1,0:T(8,128)(2,1)S(1)} %get-tuple-element.451), channel_id=1, source_target_pairs={{0,80},{8,88},{16,64},{24,72},{32,112},{40,120},{48,96},{56,104},{... | collective-permute-start | bytes 1179656 | tf_op jit(solution)/shard_map/ppermute | solution.py:24
  618.3 33.0 %collective-permute-start.10 = (bf16[1,2,64,1536]{3,2,1,0:T(8,128)(2,1)S(1)}, bf16[1,2,64,1536]{3,2,1,0:T(8,128)(2,1)S(1)}, u32[]{:S(2)}, u32[]{:S(2)}) collective-permute-start(bf16[1,2,64,1536]{3,2,1,0:T(8,128)(2,1)S(1)} %get-tuple-element.450), channel_id=1, source_target_pairs={{0,88},{8,80},{16,72},{24,64},{32,120},{40,112},{48,104},{56,96},{... | collective-permute-start | bytes 1179656 | tf_op jit(solution)/shard_map/ppermute | solution.py:24
  620.0 43.3 %collective-permute-start.11 = (bf16[1,2,64,1536]{3,2,1,0:T(8,128)(2,1)S(1)}, bf16[1,2,64,1536]{3,2,1,0:T(8,128)(2,1)S(1)}, u32[]{:S(2)}, u32[]{:S(2)}) collective-permute-start(bf16[1,2,64,1536]{3,2,1,0:T(8,128)(2,1)S(1)} %get-tuple-element.449), channel_id=1, source_target_pairs={{0,96},{8,104},{16,112},{24,120},{32,64},{40,72},{48,80},{56,88},{... | collective-permute-start | bytes 1179656 | tf_op jit(solution)/shard_map/ppermute | solution.py:24
  624.8 47.0 %collective-permute-start.12 = (bf16[1,2,64,1536]{3,2,1,0:T(8,128)(2,1)S(1)}, bf16[1,2,64,1536]{3,2,1,0:T(8,128)(2,1)S(1)}, u32[]{:S(2)}, u32[]{:S(2)}) collective-permute-start(bf16[1,2,64,1536]{3,2,1,0:T(8,128)(2,1)S(1)} %get-tuple-element.448), channel_id=1, source_target_pairs={{0,104},{8,96},{16,120},{24,112},{32,72},{40,64},{48,88},{56,80},{... | collective-permute-start | bytes 1179656 | tf_op jit(solution)/shard_map/ppermute | solution.py:24
  633.2 46.9 %collective-permute-start.13 = (bf16[1,2,64,1536]{3,2,1,0:T(8,128)(2,1)S(1)}, bf16[1,2,64,1536]{3,2,1,0:T(8,128)(2,1)S(1)}, u32[]{:S(2)}, u32[]{:S(2)}) collective-permute-start(bf16[1,2,64,1536]{3,2,1,0:T(8,128)(2,1)S(1)} %get-tuple-element.447), channel_id=1, source_target_pairs={{0,112},{8,120},{16,96},{24,104},{32,80},{40,88},{48,64},{56,72},{... | collective-permute-start | bytes 1179656 | tf_op jit(solution)/shard_map/ppermute | solution.py:24
  641.7 48.0 %collective-permute-start.14 = (bf16[1,2,64,1536]{3,2,1,0:T(8,128)(2,1)S(1)}, bf16[1,2,64,1536]{3,2,1,0:T(8,128)(2,1)S(1)}, u32[]{:S(2)}, u32[]{:S(2)}) collective-permute-start(bf16[1,2,64,1536]{3,2,1,0:T(8,128)(2,1)S(1)} %get-tuple-element.446), channel_id=1, source_target_pairs={{0,120},{8,112},{16,104},{24,96},{32,88},{40,80},{48,72},{56,64},{... | collective-permute-start | bytes 1179656 | tf_op jit(solution)/shard_map/ppermute | solution.py:24
  (20 other events, 61.0 us)
Sparse Core Ops, SparseCore 0:
  9.0 28.3 all-gather.1
  351.7 69.0 all-reduce.2
